TPU v7x, 256 devices: a whole 4x4x8 slice. The times are simulated.
256 devices in a mesh: row: 32 (over y_hi, z, core), col: 8 (over x, y_lo).
Axes of the slice: x: 4, y: 4 (y_hi: 2, y_lo: 2; y = y_hi * 2 + y_lo), z: 8, core: 2. Of those that a mesh axis runs over, the one named last changes fastest.
Arguments:
- weight: bfloat16 [16384, 16384], P('row', 'col'), may hold values from -20 to 20, as said below
- panel_index: int32 [1], replicated, may hold values from 0 to 15
Outputs:
- updated_panel: bfloat16 [16384, 1024], P('row', 'col')
- gram_rows: float32 [1024, 16384], P('row', 'col')
Inputs may be any that keep to these rules, and one draw needn't show every extreme that they name: `weight`: entries are real-valued and independent, with column and row scales that differ from column to column and row to row.
All inputs are finite; a program needn't handle non-finite values.
Results may differ from a plain program's by a relative error of at most 0.0055.
Values may be sent and summed in bfloat16 or wider, within the bound.
No kernel may reach another device: no remote copies, remote signals or barrier semaphores. Data moves between devices by JAX's collectives and lax.ppermute only.
A program may use at most 64 MiB of HBM per device.

v0:
```python
import jax
import jax.numpy as jnp
from jax import lax
from jax.sharding import PartitionSpec as P

M = 16384
PANEL = 1024


def broadcast(shard, axis, root):
    mine = lax.axis_index(axis) == root
    return lax.psum(jnp.where(mine, shard, jnp.zeros_like(shard)), axis)


def on_device(weight, panel_index):
    local_cols = weight.shape[1]
    begin_col = panel_index[0] * PANEL
    owner_col = begin_col // local_cols
    offset_col = begin_col % local_cols
    own_block = lax.dynamic_slice_in_dim(weight, offset_col, PANEL, 1)
    panel_cols = broadcast(own_block, "col", owner_col)
    inv_rows = 1.0 / M
    row_share = PANEL // lax.axis_size("row")
    totals = lax.psum(
        lax.dot_general(
            panel_cols, weight, (((0,), (0,)), ((), ())), preferred_element_type=jnp.float32
        )
        * inv_rows,
        "row",
    )
    gram_rows = lax.dynamic_slice_in_dim(totals, lax.axis_index("row") * row_share, row_share, 0)
    gram_half = totals.astype(jnp.bfloat16)
    partial_value = lax.dot_general(
        weight, gram_half, (((1,), (1,)), ((), ())), preferred_element_type=jnp.float32
    )
    summed = lax.psum_scatter(partial_value, "col", scatter_dimension=1, tiled=True)
    col_width = PANEL // lax.axis_size("col")
    own_cols = lax.dynamic_slice_in_dim(panel_cols, lax.axis_index("col") * col_width, col_width, 1)
    updated_panel = (1.5 * own_cols.astype(jnp.float32) - 0.5 * summed).astype(jnp.bfloat16)
    return (updated_panel, gram_rows)


def solution(mesh):
    placed = (P("row", "col"), P())
    return jax.shard_map(
        on_device,
        mesh=mesh,
        in_specs=placed,
        out_specs=(P("row", "col"), P("row", "col")),
        check_vma=False,
    )
```

profile of v0, /device:TPU:32, one launch (start us, length us, event | category | flops | bytes accessed | tf_op | source)
XLA Modules:
  0.0 465.9 jit_solution(5461007435810848106)
XLA Ops:
  7.2 0.0 copy-start
  7.2 0.0 all-reduce.3.cloned.1.call-start
  8.0 0.7 copy-done
  8.8 1.7 constant_dynamic-slice_fusion.1
  10.5 1.5 copy.6
  12.0 1.0 broadcast_select_fusion
  13.0 0.0 all-reduce.3.cloned.1.call-update
  13.1 0.0 all-reduce.5.cloned.1.call-start
  13.1 85.7 %all-reduce.3.cloned.1.call-done = bf16[512,1024]{0,1:T(8,128)(2,1)} async-done(((bf16[512,1024]{0,1:T(8,128)(2,1)}), bf16[512,1024]{0,1:T(8,128)(2,1)}) %all-reduce.3.cloned.1.call-update) | async-done | bytes 1048592 | tf_op jit(solution)/shard_map/psum | solution.py:12
  98.8 6.8 %convolution_multiply_fusion = f32[1024,2048]{1,0:T(8,128)} fusion(bf16[512,1024]{0,1:T(8,128)(2,1)} %all-reduce.3.cloned.1.call-done, bf16[512,2048]{1,0:T(8,128)(2,1)S(1)} %copy-done), kind=kOutput, calls=%fused_computation | convolution fusion | flops 2149580800 | bytes 11534336 | tf_op jit(solution)/shard_map/dot_general | solution.py:25
  105.6 0.0 all-reduce.5.cloned.1.call-update
  105.6 0.0 reduce-scatter.2.cloned.1.call-start
  105.7 285.7 %all-reduce.5.cloned.1.call-done = f32[1024,2048]{1,0:T(8,128)} async-done(((f32[1024,2048]{1,0:T(8,128)}), f32[1024,2048]{1,0:T(8,128)}) %all-reduce.5.cloned.1.call-update) | async-done | bytes 8388624 | tf_op jit(solution)/shard_map/psum | solution.py:24
  391.4 7.1 %fusion.2 = f32[512,1024]{0,1:T(8,128)} fusion(bf16[512,2048]{1,0:T(8,128)(2,1)S(1)} %copy-done, f32[1024,2048]{1,0:T(8,128)} %all-reduce.5.cloned.1.call-done), kind=kOutput, calls=%fused_computation.3 | convolution fusion | flops 2149580800 | bytes 12582912 | tf_op jit(solution)/shard_map/dot_general | solution.py:33
  398.5 0.0 reduce-scatter.2.cloned.1.call-update
  398.6 1.7 constant_dynamic-slice_fusion
  400.2 57.3 %reduce-scatter.2.cloned.1.call-done = f32[512,128]{0,1:T(8,128)} async-done(((f32[512,1024]{0,1:T(8,128)}), f32[512,128]{0,1:T(8,128)}) %reduce-scatter.2.cloned.1.call-update) | async-done | bytes 262160 | tf_op jit(solution)/shard_map/reduce_scatter | solution.py:36
  457.5 1.0 subtract_convert_fusion
  458.6 0.8 copy.5
Async XLA Ops:
  7.2 1.6 copy-start
  7.2 91.6 %all-reduce.3.cloned.1.call-start = ((), (), s32[]{:S(2)}) async-start(), calls=%async_computation.1 | async-start | bytes 2097152 | tf_op jit(solution)/shard_map/psum | solution.py:12
  13.1 378.4 %all-reduce.5.cloned.1.call-start = ((), (), s32[]{:S(2)}) async-start(), calls=%async_computation.2 | async-start | bytes 16777216 | tf_op jit(solution)/shard_map/psum | solution.py:24
  105.6 351.9 %reduce-scatter.2.cloned.1.call-start = ((), (), s32[]{:S(2)}) async-start(), calls=%async_computation.3 | async-start | bytes 2359296 | tf_op jit(solution)/shard_map/reduce_scatter | solution.py:36
Sparse Core Ops, SparseCore 0:
  13.2 85.5 all-reduce.2
  105.7 285.6 all-reduce.4
  398.7 58.8 reduce-scatter.1
where the time goes:
time: 466 us
  waiting for transfers between devices  429 us (92%)
  between operations  14.6 us (3%)
  matrix products  13.9 us (3%)
  local copies, waits for them, and re-layouts  6.36 us (1%)
    psum x1, waiting for transfers between devices, on_device(): lax.psum(lax.dot_general(panel_cols, weight, (((0,), (0,)), ((), ())), pr...  286 us
    psum x1, waiting for transfers between devices, broadcast(): return lax.psum(jnp.where(mine, shard, jnp.zeros_like(shard)), axis)  85.7 us
    reduce_scatter x1, waiting for transfers between devices, on_device(): lax.psum_scatter(partial_value, 'col', scatter_dimension=1, tiled=True)  57.3 us
  transfers between devices with their start and end apart: 3, of which 3 were waited for; matrix products, arithmetic and copies ran while one was open for 0% of the time, Pallas kernels for 0%

commit v1 on v0

v1 whole, which is shorter than its diff:
```python
import jax
import jax.numpy as jnp
from jax import lax
from jax.sharding import PartitionSpec as P, Mesh

M = 16384
PANEL = 1024
CFG = {"order": ("c","z","yh"), "mode": {"c":"pp","z":"pp","yh":"pp"}}

ROW = ("yh", "z", "c")
COL = ("x", "yl")


def pair_rs(x, axis):
    k = lax.axis_index(axis)
    h = x.shape[0] // 2
    keep = lax.dynamic_slice_in_dim(x, k * h, h, 0)
    send = lax.dynamic_slice_in_dim(x, (1 - k) * h, h, 0)
    return keep + lax.ppermute(send, axis, [(0, 1), (1, 0)])


def pair_ag(x, axis):
    k = lax.axis_index(axis)
    got = lax.ppermute(x, axis, [(0, 1), (1, 0)])
    return jnp.where(k == 0, jnp.concatenate([x, got], 0), jnp.concatenate([got, x], 0))


def ring_rs(x, axis):
    n = lax.axis_size(axis)
    d = lax.axis_index(axis)
    h = x.shape[0] // n
    piece = lambda k: lax.dynamic_slice_in_dim(x, (k % n) * h, h, 0)
    fw = [(i, (i + 1) % n) for i in range(n)]
    bw = [(i, (i - 1) % n) for i in range(n)]
    ncw = n // 2
    nccw = n - 1 - ncw
    acc_cw = piece(d + ncw)
    acc_ccw = piece(d - nccw)
    for s in range(ncw):
        acc_cw = lax.ppermute(acc_cw, axis, fw)
        if s < nccw:
            acc_ccw = lax.ppermute(acc_ccw, axis, bw)
        if s < ncw - 1:
            acc_cw = acc_cw + piece(d + ncw - s - 1)
        if s < nccw - 1:
            acc_ccw = acc_ccw + piece(d - nccw + s + 1)
    return acc_cw + acc_ccw + piece(d)


def ring_ag(x, axis):
    n = lax.axis_size(axis)
    d = lax.axis_index(axis)
    h = x.shape[0]
    fw = [(i, (i + 1) % n) for i in range(n)]
    bw = [(i, (i - 1) % n) for i in range(n)]
    out = jnp.zeros((n * h,) + x.shape[1:], x.dtype)
    out = lax.dynamic_update_slice_in_dim(out, x, d * h, 0)
    ncw = n // 2
    nccw = n - 1 - ncw
    a = x
    b = x
    for s in range(ncw):
        a = lax.ppermute(a, axis, fw)
        out = lax.dynamic_update_slice_in_dim(out, a, ((d - s - 1) % n) * h, 0)
        if s < nccw:
            b = lax.ppermute(b, axis, bw)
            out = lax.dynamic_update_slice_in_dim(out, b, ((d + s + 1) % n) * h, 0)
    return out


def rs(x, axis, mode):
    if mode == "sc":
        return lax.psum_scatter(x, axis, scatter_dimension=0, tiled=True)
    if lax.axis_size(axis) == 2:
        return pair_rs(x, axis)
    return ring_rs(x, axis)


def ag(x, axis, mode):
    if mode == "sc":
        return lax.all_gather(x, axis, axis=0, tiled=True)
    if lax.axis_size(axis) == 2:
        return pair_ag(x, axis)
    return ring_ag(x, axis)


def broadcast(shard, root):
    mine = lax.axis_index(COL) == root
    t = jnp.where(mine, shard, jnp.zeros_like(shard)).T
    t = rs(t, "x", "pp")
    t = rs(t, "yl", "pp")
    t = ag(t, "yl", "pp")
    t = ag(t, "x", "pp")
    return t.T


def on_device(weight, panel_index):
    local_cols = weight.shape[1]
    begin_col = panel_index[0] * PANEL
    owner_col = begin_col // local_cols
    offset_col = begin_col % local_cols
    own_block = lax.dynamic_slice_in_dim(weight, offset_col, PANEL, 1)
    panel_cols = broadcast(own_block, owner_col)
    order = CFG["order"]
    sizes = {a: lax.axis_size(a) for a in ROW}
    shape = [sizes[a] for a in ROW] + [PANEL // lax.axis_size(ROW)]
    perm = [ROW.index(a) for a in order] + [3]
    p5 = panel_cols.reshape((panel_cols.shape[0],) + tuple(shape))
    p_perm = jnp.transpose(p5, [0] + [q + 1 for q in perm]).reshape(panel_cols.shape)
    part = lax.dot_general(p_perm, weight, (((0,), (0,)), ((), ())), preferred_element_type=jnp.float32) * (1.0 / M)
    x = part
    for a in order:
        x = rs(x, a, CFG["mode"][a])
    gram_rows = x
    g = gram_rows.astype(jnp.bfloat16)
    for a in reversed(order):
        g = ag(g, a, CFG["mode"][a])
    inv = [perm.index(q) for q in range(4)]
    g5 = g.reshape(tuple(shape[q] for q in perm) + (g.shape[1],))
    gram_half = jnp.transpose(g5, inv + [4]).reshape(g.shape)
    partial_t = lax.dot_general(gram_half, weight, (((1,), (1,)), ((), ())), preferred_element_type=jnp.float32)
    summed = rs(rs(partial_t, "x", "pp"), "yl", "pp").T
    col_width = PANEL // lax.axis_size(COL)
    own_cols = lax.dynamic_slice_in_dim(panel_cols, lax.axis_index(COL) * col_width, col_width, 1)
    updated_panel = (1.5 * own_cols.astype(jnp.float32) - 0.5 * summed).astype(jnp.bfloat16)
    return (updated_panel, gram_rows)


def solution(mesh):
    m5 = Mesh(mesh.devices.reshape(2, 8, 2, 4, 2), ROW + COL)
    return jax.shard_map(on_device, mesh=m5, in_specs=(P(ROW, COL), P()),
                         out_specs=(P(ROW, COL), P(ROW, COL)), check_vma=False)
```

time: 466 us -> 257 us (0.55)
  waiting for transfers between devices: 429 us -> 156 us
  starting transfers between devices: 0.12 us -> 39.2 us
  other arithmetic: 2.07 us -> 26.1 us
  local copies, waits for them, and re-layouts: 6.36 us -> 25.9 us
  between operations: 14.6 us -> 1.73 us
  matrix products: 13.9 us -> 4.71 us
    psum x2 -> x0, waiting for transfers between devices: 371 us -> none  [the longest x1 286 us: on_device(): lax.psum(lax.dot_general(panel_cols, weight, (((0,), (0,)), ((), ())), pr...]
    ppermute x0 -> x30, waiting for transfers between devices: none -> 156 us  [the longest x8 84.8 us: ring_rs(): acc_cw = lax.ppermute(acc_cw, axis, fw)]
    reduce_scatter x1 -> x0, waiting for transfers between devices: 57.3 us -> none  [on_device(): lax.psum_scatter(partial_value, 'col', scatter_dimension=1, tiled=True)]
    ppermute x0 -> x30, starting transfers between devices: none -> 39.2 us  [the longest x8 11.1 us: ring_rs(): acc_cw = lax.ppermute(acc_cw, axis, fw)]
    add x0 -> x8, other arithmetic: none -> 13.2 us  [the longest x2 5.29 us: ring_rs(): acc_ccw = acc_ccw + piece(d - nccw + s + 1)]
    dot_general x2, matrix products: 13.9 us -> 4.71 us  [the longest x1 2.36 us: on_device(): lax.dot_general(gram_half, weight, (((1,), (1,)), ((), ())), preferred_el...]
    dynamic_update_slice x0 -> x10, local copies, waits for them, and re-layouts: none -> 8.01 us  [the longest x6 4.86 us: ring_ag(): out = lax.dynamic_update_slice_in_dim(out, a, (d - s - 1) % n * h, 0)]
    unnamed x4 -> x12, local copies, waits for them, and re-layouts: 2.99 us -> 8.67 us
  transfers between devices with their start and end apart: 3 -> 30, of which waited for: 3 -> 24; matrix products, arithmetic and copies ran while one was open for 0% -> 3% of each run, Pallas kernels for 0% -> 0%
where the time goes in v1:
time: 257 us; the launch traced here: 254 us
  waiting for transfers between devices  156 us (61%)
  starting transfers between devices  39.2 us (15%)
  other arithmetic  26.1 us (10%)
  local copies, waits for them, and re-layouts  25.9 us (10%)
  matrix products  4.71 us (2%)
    ppermute x8, waiting for transfers between devices, ring_rs(): acc_cw = lax.ppermute(acc_cw, axis, fw)  84.8 us
    ppermute x6, waiting for transfers between devices, ring_ag(): a = lax.ppermute(a, axis, fw)  33.8 us
    ppermute x4, waiting for transfers between devices, pair_rs(): return keep + lax.ppermute(send, axis, [(0, 1), (1, 0)])  21.2 us
    ppermute x3, waiting for transfers between devices, pair_ag(): got = lax.ppermute(x, axis, [(0, 1), (1, 0)])  11.2 us
    ppermute x8, starting transfers between devices, ring_rs(): acc_cw = lax.ppermute(acc_cw, axis, fw)  11.1 us
    unnamed x12, local copies, waits for them, and re-layouts  8.67 us
    ppermute x5, starting transfers between devices, ring_rs(): acc_ccw = lax.ppermute(acc_ccw, axis, bw)  7.56 us
    ppermute x4, starting transfers between devices, ring_ag(): b = lax.ppermute(b, axis, bw)  6.67 us
  transfers between devices with their start and end apart: 30, of which 24 were waited for; matrix products, arithmetic and copies ran while one was open for 3% of the time, Pallas kernels for 0%

profile of v1, /device:TPU:32, one launch (start us, length us, event | category | flops | bytes accessed | tf_op | source)
XLA Modules:
  0.0 253.7 jit_solution(13862159195962495115)
XLA Ops:
  10.9 6.0 %collective-permute-done = bf16[256,512]{1,0:T(8,128)(2,1)S(1)} collective-permute-done((bf16[256,512]{1,0:T(8,128)(2,1)S(1)}, bf16[256,512]{1,0:T(8,128)(2,1)S(1)}, u32[]{:S(2)}, u32[]{:S(2)}) %collective-permute-start) | collective-permute-done | bytes 262176 | tf_op jit(solution)/shard_map/ppermute | solution.py:40
  18.3 8.1 %collective-permute-done.1 = bf16[256,512]{1,0:T(8,128)(2,1)S(1)} collective-permute-done((bf16[256,512]{1,0:T(8,128)(2,1)S(1)}, bf16[256,512]{1,0:T(8,128)(2,1)S(1)}, u32[]{:S(2)}, u32[]{:S(2)}) %collective-permute-start.1) | collective-permute-done | bytes 262176 | tf_op jit(solution)/shard_map/ppermute | solution.py:40
  29.2 3.7 %collective-permute-done.3 = bf16[128,512]{1,0:T(8,128)(2,1)S(1)} collective-permute-done((bf16[128,512]{1,0:T(8,128)(2,1)S(1)}, bf16[128,512]{1,0:T(8,128)(2,1)S(1)}, u32[]{:S(2)}, u32[]{:S(2)}) %collective-permute-start.3) | collective-permute-done | bytes 131104 | tf_op jit(solution)/shard_map/ppermute | solution.py:19
  34.6 3.4 %collective-permute-done.4 = bf16[128,512]{1,0:T(8,128)(2,1)S(1)} collective-permute-done((bf16[128,512]{1,0:T(8,128)(2,1)S(1)}, bf16[128,512]{1,0:T(8,128)(2,1)S(1)}, u32[]{:S(2)}, u32[]{:S(2)}) %collective-permute-start.4) | collective-permute-done | bytes 131104 | tf_op jit(solution)/shard_map/ppermute | solution.py:24
  42.1 6.1 %collective-permute-done.5 = bf16[256,512]{1,0:T(8,128)(2,1)S(1)} collective-permute-done((bf16[256,512]{1,0:T(8,128)(2,1)}, bf16[256,512]{1,0:T(8,128)(2,1)S(1)}, u32[]{:S(2)}, u32[]{:S(2)}) %collective-permute-start.5) | collective-permute-done | bytes 262176 | tf_op jit(solution)/shard_map/ppermute | solution.py:63
  49.2 6.7 %collective-permute-done.7 = bf16[256,512]{1,0:T(8,128)(2,1)} collective-permute-done((bf16[256,512]{1,0:T(8,128)(2,1)S(1)}, bf16[256,512]{1,0:T(8,128)(2,1)}, u32[]{:S(2)}, u32[]{:S(2)}) %collective-permute-start.7) | collective-permute-done | bytes 262176 | tf_op jit(solution)/shard_map/ppermute | solution.py:63
  63.8 7.5 %collective-permute-done.8 = f32[512,2048]{1,0:T(8,128)} collective-permute-done((f32[512,2048]{1,0:T(8,128)}, f32[512,2048]{1,0:T(8,128)}, u32[]{:S(2)}, u32[]{:S(2)}) %collective-permute-start.8) | collective-permute-done | bytes 4194336 | tf_op jit(solution)/shard_map/ppermute | solution.py:19
  71.3 4.2 %dynamic-slice_add_fusion = f32[512,2048]{1,0:T(8,128)S(1)} fusion(f32[512,2048]{1,0:T(8,128)} %collective-permute-done.8, f32[1024,2048]{1,0:T(8,128)} %copy-done.2, s32[]{:T(128)S(6)} %select_n.236), kind=kLoop, calls=%fused_computation.2 | loop fusion | flops 1048576 | bytes 12582916 | tf_op jit(solution)/shard_map/add | solution.py:19
  80.3 12.4 %collective-permute-done.9 = f32[64,2048]{1,0:T(8,128)} collective-permute-done((f32[64,2048]{1,0:T(8,128)}, f32[64,2048]{1,0:T(8,128)}, u32[]{:S(2)}, u32[]{:S(2)}) %collective-permute-start.9) | collective-permute-done | bytes 524320 | tf_op jit(solution)/shard_map/ppermute | solution.py:40
  99.4 12.0 %collective-permute-done.10 = f32[64,2048]{1,0:T(8,128)} collective-permute-done((f32[64,2048]{1,0:T(8,128)}, f32[64,2048]{1,0:T(8,128)}, u32[]{:S(2)}, u32[]{:S(2)}) %collective-permute-start.10) | collective-permute-done | bytes 524320 | tf_op jit(solution)/shard_map/ppermute | solution.py:40
  114.0 3.4 %collective-permute-start.11 = (f32[64,2048]{1,0:T(8,128)}, f32[64,2048]{1,0:T(8,128)}, u32[]{:S(2)}, u32[]{:S(2)}) collective-permute-start(f32[64,2048]{1,0:T(8,128)} %get-tuple-element.17), channel_id=1, source_target_pairs={{0,16},{16,32},{32,48},{48,64},{64,80},{80,96},{96,112},{112,0},{1... | collective-permute-start | bytes 1572872 | tf_op jit(solution)/shard_map/ppermute | solution.py:40
  117.4 10.7 %collective-permute-done.11 = f32[64,2048]{1,0:T(8,128)} collective-permute-done((f32[64,2048]{1,0:T(8,128)}, f32[64,2048]{1,0:T(8,128)}, u32[]{:S(2)}, u32[]{:S(2)}) %collective-permute-start.11) | collective-permute-done | bytes 524320 | tf_op jit(solution)/shard_map/ppermute | solution.py:40
  135.3 9.4 %collective-permute-done.12 = f32[64,2048]{1,0:T(8,128)} collective-permute-done((f32[64,2048]{1,0:T(8,128)}, f32[64,2048]{1,0:T(8,128)}, u32[]{:S(2)}, u32[]{:S(2)}) %collective-permute-start.12) | collective-permute-done | bytes 524320 | tf_op jit(solution)/shard_map/ppermute | solution.py:40
  152.3 4.9 %collective-permute-done.16 = f32[32,2048]{1,0:T(8,128)S(1)} collective-permute-done((f32[32,2048]{1,0:T(8,128)}, f32[32,2048]{1,0:T(8,128)S(1)}, u32[]{:S(2)}, u32[]{:S(2)}) %collective-permute-start.16) | collective-permute-done | bytes 262176 | tf_op jit(solution)/shard_map/ppermute | solution.py:19
  162.1 3.3 %collective-permute-done.17 = bf16[32,2048]{1,0:T(8,128)(2,1)S(1)} collective-permute-done((bf16[32,2048]{1,0:T(8,128)(2,1)S(1)}, bf16[32,2048]{1,0:T(8,128)(2,1)S(1)}, u32[]{:S(2)}, u32[]{:S(2)}) %collective-permute-start.17) | collective-permute-done | bytes 131104 | tf_op jit(solution)/shard_map/ppermute | solution.py:24
  169.9 6.9 %collective-permute-done.18 = bf16[64,2048]{1,0:T(8,128)(2,1)} collective-permute-done((bf16[64,2048]{1,0:T(8,128)(2,1)}, bf16[64,2048]{1,0:T(8,128)(2,1)}, u32[]{:S(2)}, u32[]{:S(2)}) %collective-permute-start.18) | collective-permute-done | bytes 262176 | tf_op jit(solution)/shard_map/ppermute | solution.py:63
  181.2 4.2 %collective-permute-done.20 = bf16[64,2048]{1,0:T(8,128)(2,1)S(1)} collective-permute-done((bf16[64,2048]{1,0:T(8,128)(2,1)}, bf16[64,2048]{1,0:T(8,128)(2,1)S(1)}, u32[]{:S(2)}, u32[]{:S(2)}) %collective-permute-start.20) | collective-permute-done | bytes 262176 | tf_op jit(solution)/shard_map/ppermute | solution.py:63
  189.8 4.1 %collective-permute-done.22 = bf16[64,2048]{1,0:T(8,128)(2,1)S(1)} collective-permute-done((bf16[64,2048]{1,0:T(8,128)(2,1)S(1)}, bf16[64,2048]{1,0:T(8,128)(2,1)S(1)}, u32[]{:S(2)}, u32[]{:S(2)}) %collective-permute-start.22) | collective-permute-done | bytes 262176 | tf_op jit(solution)/shard_map/ppermute | solution.py:63
  195.4 5.9 %collective-permute-done.24 = bf16[64,2048]{1,0:T(8,128)(2,1)S(1)} collective-permute-done((bf16[64,2048]{1,0:T(8,128)(2,1)S(1)}, bf16[64,2048]{1,0:T(8,128)(2,1)S(1)}, u32[]{:S(2)}, u32[]{:S(2)}) %collective-permute-start.24) | collective-permute-done | bytes 262176 | tf_op jit(solution)/shard_map/ppermute | solution.py:63
  202.0 4.5 %collective-permute-done.25 = bf16[512,2048]{1,0:T(8,128)(2,1)} collective-permute-done((bf16[512,2048]{1,0:T(8,128)(2,1)}, bf16[512,2048]{1,0:T(8,128)(2,1)}, u32[]{:S(2)}, u32[]{:S(2)}) %collective-permute-start.25) | collective-permute-done | bytes 2097184 | tf_op jit(solution)/shard_map/ppermute | solution.py:24
  206.5 4.7 %maximum_select_fusion = bf16[1024,2048]{1,0:T(8,128)(2,1)S(1)} fusion(bf16[512,2048]{1,0:T(8,128)(2,1)} %collective-permute-done.25, bf16[512,2048]{1,0:T(8,128)(2,1)} %constant_dynamic-update-slice_fusion, pred[]{:T(512)S(6)} %eq.42), kind=kLoop, calls=%fused_computation.1 | loop fusion | flops 18874368 | bytes 8388609 | tf_op jit(solution)/shard_map/jit(_where)/select_n | solution.py:25
  214.3 15.2 %collective-permute-done.26 = f32[256,512]{1,0:T(8,128)S(1)} collective-permute-done((f32[256,512]{1,0:T(8,128)S(1)}, f32[256,512]{1,0:T(8,128)S(1)}, u32[]{:S(2)}, u32[]{:S(2)}) %collective-permute-start.26) | collective-permute-done | bytes 524320 | tf_op jit(solution)/shard_map/ppermute | solution.py:40
  233.0 11.1 %collective-permute-done.27 = f32[256,512]{1,0:T(8,128)S(1)} collective-permute-done((f32[256,512]{1,0:T(8,128)S(1)}, f32[256,512]{1,0:T(8,128)S(1)}, u32[]{:S(2)}, u32[]{:S(2)}) %collective-permute-start.27) | collective-permute-done | bytes 524320 | tf_op jit(solution)/shard_map/ppermute | solution.py:40
  246.7 5.2 %collective-permute-done.29 = f32[128,512]{1,0:T(8,128)} collective-permute-done((f32[128,512]{1,0:T(8,128)S(1)}, f32[128,512]{1,0:T(8,128)}, u32[]{:S(2)}, u32[]{:S(2)}) %collective-permute-start.29) | collective-permute-done | bytes 262176 | tf_op jit(solution)/shard_map/ppermute | solution.py:19
  (88 shorter events, 88.6 us)
Async XLA Ops:
  7.6 9.3 %collective-permute-start = (bf16[256,512]{1,0:T(8,128)(2,1)S(1)}, bf16[256,512]{1,0:T(8,128)(2,1)S(1)}, u32[]{:S(2)}, u32[]{:S(2)}) collective-permute-start(bf16[256,512]{1,0:T(8,128)(2,1)S(1)} %get-tuple-element.23), channel_id=1, source_target_pairs={{0,2},{2,4},{4,6},{6,0},{1,3},{3,5},{5,7},{7,1},{8,10},{10,12},{12... | collective-permute-start | bytes 786440 | tf_op jit(solution)/shard_map/ppermute | solution.py:40
  9.2 9.1 %collective-permute-start.2 = (bf16[256,512]{1,0:T(8,128)(2,1)S(1)}, bf16[256,512]{1,0:T(8,128)(2,1)S(1)}, u32[]{:S(2)}, u32[]{:S(2)}) collective-permute-start(bf16[256,512]{1,0:T(8,128)(2,1)S(1)} %get-tuple-element.22), channel_id=1, source_target_pairs={{0,6},{2,0},{4,2},{6,4},{1,7},{3,1},{5,3},{7,5},{8,14},{10,8},{12,... | collective-permute-start | bytes 786440 | tf_op jit(solution)/shard_map/ppermute | solution.py:42
  18.0 8.5 %collective-permute-start.1 = (bf16[256,512]{1,0:T(8,128)(2,1)S(1)}, bf16[256,512]{1,0:T(8,128)(2,1)S(1)}, u32[]{:S(2)}, u32[]{:S(2)}) collective-permute-start(bf16[256,512]{1,0:T(8,128)(2,1)S(1)} %bitcast_add_fusion.1), channel_id=1, source_target_pairs={{0,2},{2,4},{4,6},{6,0},{1,3},{3,5},{5,7},{7,1},{8,10},{10,12},{12... | collective-permute-start | bytes 786440 | tf_op jit(solution)/shard_map/ppermute | solution.py:40
  38.8 9.3 %collective-permute-start.5 = (bf16[256,512]{1,0:T(8,128)(2,1)}, bf16[256,512]{1,0:T(8,128)(2,1)S(1)}, u32[]{:S(2)}, u32[]{:S(2)}) collective-permute-start(bf16[256,512]{1,0:T(8,128)(2,1)} %get-tuple-element.13), channel_id=1, source_target_pairs={{0,2},{2,4},{4,6},{6,0},{1,3},{3,5},{5,7},{7,1},{8,10},{10,12},{12... | collective-permute-start | bytes 786440 | tf_op jit(solution)/shard_map/ppermute | solution.py:63
  38.8 9.3 %collective-permute-start.6 = (bf16[256,512]{1,0:T(8,128)(2,1)}, bf16[256,512]{1,0:T(8,128)(2,1)}, u32[]{:S(2)}, u32[]{:S(2)}) collective-permute-start(bf16[256,512]{1,0:T(8,128)(2,1)} %get-tuple-element.13), channel_id=1, source_target_pairs={{0,6},{2,0},{4,2},{6,4},{1,7},{3,1},{5,3},{7,5},{8,14},{10,8},{12,... | collective-permute-start | bytes 786440 | tf_op jit(solution)/shard_map/ppermute | solution.py:66
  48.1 7.7 %collective-permute-start.7 = (bf16[256,512]{1,0:T(8,128)(2,1)S(1)}, bf16[256,512]{1,0:T(8,128)(2,1)}, u32[]{:S(2)}, u32[]{:S(2)}) collective-permute-start(bf16[256,512]{1,0:T(8,128)(2,1)S(1)} %collective-permute-done.5), channel_id=1, source_target_pairs={{0,2},{2,4},{4,6},{6,0},{1,3},{3,5},{5,7},{7,1},{8,10},{10,12},{12... | collective-permute-start | bytes 786440 | tf_op jit(solution)/shard_map/ppermute | solution.py:63
  63.8 7.5 %collective-permute-start.8 = (f32[512,2048]{1,0:T(8,128)}, f32[512,2048]{1,0:T(8,128)}, u32[]{:S(2)}, u32[]{:S(2)}) collective-permute-start(f32[512,2048]{1,0:T(8,128)} %constant_dynamic-slice_fusion.5), channel_id=1, source_target_pairs={{0,8},{8,0},{1,9},{9,1},{2,10},{10,2},{3,11},{11,3},{4,12},{12,4},... | collective-permute-start | bytes 12582920 | tf_op jit(solution)/shard_map/ppermute | solution.py:19
  78.4 14.3 %collective-permute-start.9 = (f32[64,2048]{1,0:T(8,128)}, f32[64,2048]{1,0:T(8,128)}, u32[]{:S(2)}, u32[]{:S(2)}) collective-permute-start(f32[64,2048]{1,0:T(8,128)} %constant_dynamic-slice_fusion.4), channel_id=1, source_target_pairs={{0,16},{16,32},{32,48},{48,64},{64,80},{80,96},{96,112},{112,0},{1... | collective-permute-start | bytes 1572872 | tf_op jit(solution)/shard_map/ppermute | solution.py:40
  95.1 16.2 %collective-permute-start.10 = (f32[64,2048]{1,0:T(8,128)}, f32[64,2048]{1,0:T(8,128)}, u32[]{:S(2)}, u32[]{:S(2)}) collective-permute-start(f32[64,2048]{1,0:T(8,128)} %get-tuple-element.19), channel_id=1, source_target_pairs={{0,16},{16,32},{32,48},{48,64},{64,80},{80,96},{96,112},{112,0},{1... | collective-permute-start | bytes 1572872 | tf_op jit(solution)/shard_map/ppermute | solution.py:40
  97.1 14.3 %collective-permute-start.13 = (f32[64,2048]{1,0:T(8,128)}, f32[64,2048]{1,0:T(8,128)}, u32[]{:S(2)}, u32[]{:S(2)}) collective-permute-start(f32[64,2048]{1,0:T(8,128)} %get-tuple-element.18), channel_id=1, source_target_pairs={{0,112},{16,0},{32,16},{48,32},{64,48},{80,64},{96,80},{112,96},{1... | collective-permute-start | bytes 1572872 | tf_op jit(solution)/shard_map/ppermute | solution.py:42
  114.0 14.1 %collective-permute-start.11 = (f32[64,2048]{1,0:T(8,128)}, f32[64,2048]{1,0:T(8,128)}, u32[]{:S(2)}, u32[]{:S(2)}) collective-permute-start(f32[64,2048]{1,0:T(8,128)} %get-tuple-element.17), channel_id=1, source_target_pairs={{0,16},{16,32},{32,48},{48,64},{64,80},{80,96},{96,112},{112,0},{1... | collective-permute-start | bytes 1572872 | tf_op jit(solution)/shard_map/ppermute | solution.py:40
  117.4 13.2 %collective-permute-start.14 = (f32[64,2048]{1,0:T(8,128)}, f32[64,2048]{1,0:T(8,128)}, u32[]{:S(2)}, u32[]{:S(2)}) collective-permute-start(f32[64,2048]{1,0:T(8,128)} %get-tuple-element.16), channel_id=1, source_target_pairs={{0,112},{16,0},{32,16},{48,32},{64,48},{80,64},{96,80},{112,96},{1... | collective-permute-start | bytes 1572872 | tf_op jit(solution)/shard_map/ppermute | solution.py:42
  133.2 11.4 %collective-permute-start.12 = (f32[64,2048]{1,0:T(8,128)}, f32[64,2048]{1,0:T(8,128)}, u32[]{:S(2)}, u32[]{:S(2)}) collective-permute-start(f32[64,2048]{1,0:T(8,128)} %get-tuple-element.15), channel_id=1, source_target_pairs={{0,16},{16,32},{32,48},{48,64},{64,80},{80,96},{96,112},{112,0},{1... | collective-permute-start | bytes 1572872 | tf_op jit(solution)/shard_map/ppermute | solution.py:40
  135.0 11.2 %collective-permute-start.15 = (f32[64,2048]{1,0:T(8,128)}, f32[64,2048]{1,0:T(8,128)}, u32[]{:S(2)}, u32[]{:S(2)}) collective-permute-start(f32[64,2048]{1,0:T(8,128)} %get-tuple-element.14), channel_id=1, source_target_pairs={{0,112},{16,0},{32,16},{48,32},{64,48},{80,64},{96,80},{112,96},{1... | collective-permute-start | bytes 1572872 | tf_op jit(solution)/shard_map/ppermute | solution.py:42
  149.1 8.1 %collective-permute-start.16 = (f32[32,2048]{1,0:T(8,128)}, f32[32,2048]{1,0:T(8,128)S(1)}, u32[]{:S(2)}, u32[]{:S(2)}) collective-permute-start(f32[32,2048]{1,0:T(8,128)} %constant_dynamic-slice_fusion.2), channel_id=1, source_target_pairs={{0,128},{128,0},{1,129},{129,1},{2,130},{130,2},{3,131},{131,3},{4... | collective-permute-start | bytes 786440 | tf_op jit(solution)/shard_map/ppermute | solution.py:19
  167.8 8.9 %collective-permute-start.18 = (bf16[64,2048]{1,0:T(8,128)(2,1)}, bf16[64,2048]{1,0:T(8,128)(2,1)}, u32[]{:S(2)}, u32[]{:S(2)}) collective-permute-start(bf16[64,2048]{1,0:T(8,128)(2,1)} %get-tuple-element.9), channel_id=1, source_target_pairs={{0,16},{16,32},{32,48},{48,64},{64,80},{80,96},{96,112},{112,0},{1... | collective-permute-start | bytes 786440 | tf_op jit(solution)/shard_map/ppermute | solution.py:63
  169.6 9.6 %collective-permute-start.19 = (bf16[64,2048]{1,0:T(8,128)(2,1)}, bf16[64,2048]{1,0:T(8,128)(2,1)S(1)}, u32[]{:S(2)}, u32[]{:S(2)}) collective-permute-start(bf16[64,2048]{1,0:T(8,128)(2,1)} %get-tuple-element.9), channel_id=1, source_target_pairs={{0,112},{16,0},{32,16},{48,32},{64,48},{80,64},{96,80},{112,96},{1... | collective-permute-start | bytes 786440 | tf_op jit(solution)/shard_map/ppermute | solution.py:66
  176.7 8.7 %collective-permute-start.20 = (bf16[64,2048]{1,0:T(8,128)(2,1)}, bf16[64,2048]{1,0:T(8,128)(2,1)S(1)}, u32[]{:S(2)}, u32[]{:S(2)}) collective-permute-start(bf16[64,2048]{1,0:T(8,128)(2,1)} %collective-permute-done.18), channel_id=1, source_target_pairs={{0,16},{16,32},{32,48},{48,64},{64,80},{80,96},{96,112},{112,0},{1... | collective-permute-start | bytes 786440 | tf_op jit(solution)/shard_map/ppermute | solution.py:63
  179.2 8.0 %collective-permute-start.21 = (bf16[64,2048]{1,0:T(8,128)(2,1)S(1)}, bf16[64,2048]{1,0:T(8,128)(2,1)S(1)}, u32[]{:S(2)}, u32[]{:S(2)}) collective-permute-start(bf16[64,2048]{1,0:T(8,128)(2,1)S(1)} %collective-permute-done.19), channel_id=1, source_target_pairs={{0,112},{16,0},{32,16},{48,32},{64,48},{80,64},{96,80},{112,96},{1... | collective-permute-start | bytes 786440 | tf_op jit(solution)/shard_map/ppermute | solution.py:66
  185.4 8.5 %collective-permute-start.22 = (bf16[64,2048]{1,0:T(8,128)(2,1)S(1)}, bf16[64,2048]{1,0:T(8,128)(2,1)S(1)}, u32[]{:S(2)}, u32[]{:S(2)}) collective-permute-start(bf16[64,2048]{1,0:T(8,128)(2,1)S(1)} %collective-permute-done.20), channel_id=1, source_target_pairs={{0,16},{16,32},{32,48},{48,64},{64,80},{80,96},{96,112},{112,0},{1... | collective-permute-start | bytes 786440 | tf_op jit(solution)/shard_map/ppermute | solution.py:63
  187.2 7.5 %collective-permute-start.23 = (bf16[64,2048]{1,0:T(8,128)(2,1)S(1)}, bf16[64,2048]{1,0:T(8,128)(2,1)S(1)}, u32[]{:S(2)}, u32[]{:S(2)}) collective-permute-start(bf16[64,2048]{1,0:T(8,128)(2,1)S(1)} %collective-permute-done.21), channel_id=1, source_target_pairs={{0,112},{16,0},{32,16},{48,32},{64,48},{80,64},{96,80},{112,96},{1... | collective-permute-start | bytes 786440 | tf_op jit(solution)/shard_map/ppermute | solution.py:66
  214.3 15.3 %collective-permute-start.26 = (f32[256,512]{1,0:T(8,128)S(1)}, f32[256,512]{1,0:T(8,128)S(1)}, u32[]{:S(2)}, u32[]{:S(2)}) collective-permute-start(f32[256,512]{1,0:T(8,128)S(1)} %constant_dynamic-slice_fusion.1), channel_id=1, source_target_pairs={{0,2},{2,4},{4,6},{6,0},{1,3},{3,5},{5,7},{7,1},{8,10},{10,12},{12... | collective-permute-start | bytes 1572872 | tf_op jit(solution)/shard_map/ppermute | solution.py:40
  229.7 14.4 %collective-permute-start.27 = (f32[256,512]{1,0:T(8,128)S(1)}, f32[256,512]{1,0:T(8,128)S(1)}, u32[]{:S(2)}, u32[]{:S(2)}) collective-permute-start(f32[256,512]{1,0:T(8,128)S(1)} %get-tuple-element.21), channel_id=1, source_target_pairs={{0,2},{2,4},{4,6},{6,0},{1,3},{3,5},{5,7},{7,1},{8,10},{10,12},{12... | collective-permute-start | bytes 1572872 | tf_op jit(solution)/shard_map/ppermute | solution.py:40
  229.7 14.3 %collective-permute-start.28 = (f32[256,512]{1,0:T(8,128)S(1)}, f32[256,512]{1,0:T(8,128)S(1)}, u32[]{:S(2)}, u32[]{:S(2)}) collective-permute-start(f32[256,512]{1,0:T(8,128)S(1)} %get-tuple-element.20), channel_id=1, source_target_pairs={{0,6},{2,0},{4,2},{6,4},{1,7},{3,1},{5,3},{7,5},{8,14},{10,8},{12,... | collective-permute-start | bytes 1572872 | tf_op jit(solution)/shard_map/ppermute | solution.py:42
  (11 other events, 45.2 us)
